TPU v7x, 32 devices: a whole 2x2x4 slice. The times are simulated.
32 devices in a mesh: groups: 2 (over y), cols: 4 (over z), slab: 2 (over x), rep: 2 (over core).
Axes of the slice: x: 2, y: 2, z: 4, core: 2. Of those that a mesh axis runs over, the one named last changes fastest.
Arguments:
- fields: bfloat16 [16, 8, 2048, 512], P('cols', 'groups', 'rep', 'slab'), parts along dimension 1, may hold values from -250 to 250
- stresses: bfloat16 [6, 8, 512, 128], P(None, 'groups', 'rep', 'slab'), parts along dimension 1, may hold values from -750 to 750
- planes: int32 [8], P('groups'), parts along dimension 0, may hold values from 0 to 2047, as said below
- active_masks: int32 [3, 6, 256], replicated, may hold values 0 or 1
Outputs:
- coefficients: float32 [3, 12, 256], P(None, 'groups', 'cols'), parts along dimension 1
- misfit: bfloat16 [6, 8, 512, 128], P(None, 'groups', 'rep', 'slab'), parts along dimension 1
There are 2 independent parts, one for each index of `groups`. A program takes and returns all parts, laid end to end along the dimension named above; an argument that names none is the same for every part. Nothing has to cross between parts.
Inputs may be any that keep to these rules, and one draw needn't show every extreme that they name: `planes`: sorted and distinct; either the first is 0 or the last is 2047.
All inputs are finite; a program needn't handle non-finite values.
Results may differ from a plain program's by a relative error of at most 0.0069.
Values may be sent and summed in bfloat16 or wider, within the bound.
No kernel may reach another device: no remote copies, remote signals or barrier semaphores. Data moves between devices by JAX's collectives and lax.ppermute only.
A program may use at most 128 MiB of HBM per device.

v0:
```python
import math
import jax
import jax.numpy as jnp
import numpy as np
from jax import lax
from jax.sharding import PartitionSpec as P

STRESS = 6
TERMS = 256
NY = 2048
PASSES = 3
ITERS = 3
ridge_weight = 0.05
epsilon = 1e-06


def extended(array, sides, width):
    for axis, dim in sides:
        count, length = (lax.axis_size(axis), array.shape[dim])
        up = [(i, (i + 1) % count) for i in range(count)]
        down = [(j, i) for i, j in up]
        last = lax.slice_in_dim(array, length - width, length, axis=dim)
        leading = lax.slice_in_dim(array, 0, width, axis=dim)
        before = lax.ppermute(last, axis, up)
        after = lax.ppermute(leading, axis, down)
        array = jnp.concatenate([before, array, after], axis=dim)
    return array


def kernel(spread):
    offsets = np.arange(13) - 6.0
    values = np.exp(-offsets * offsets / (2.0 * spread * spread))
    return values / values.sum()


def filter_table(cells, first_taps, second_taps):
    out_count = cells // 4
    table = np.zeros((cells + 10, 2, out_count), np.float32)
    for which, taps in ((0, first_taps), (1, second_taps)):
        for out_index in range(out_count):
            for tap_index in range(13):
                table[1 + tap_index + 4 * out_index, which, out_index] = taps[tap_index]
    return table


def library(narrow_part, broad_part):
    product = (
        narrow_part.astype(jnp.float32)[:, None, :] * broad_part.astype(jnp.float32)[None, :, :]
    )
    return product.astype(jnp.bfloat16).reshape(
        narrow_part.shape[0] * broad_part.shape[0], narrow_part.shape[1]
    )


def local(fields, stresses, planes, active_masks):
    chan_dev, plane_count, cells_x, cells_z = fields.shape
    coarse_x = cells_x // 4
    coarse_z = cells_z // 4
    row_count = plane_count * coarse_x * coarse_z
    col_devices = lax.axis_size("cols")
    column_index = lax.axis_index("cols")
    term_dev = TERMS // col_devices
    offset = column_index * term_dev
    samples = float(row_count * lax.axis_size("slab") * lax.axis_size("rep"))
    height = 2.0 * (planes.astype(jnp.float32) + 0.5) / NY - 1.0
    root_weight = jnp.sqrt(1.2 - height * height)
    padded = extended(fields, (("slab", 3), ("rep", 2)), 5)
    widened = padded.astype(jnp.float32)
    narrow_taps = kernel(1.5)
    broad_taps = kernel(3.0)
    span_table = jnp.asarray(filter_table(cells_z, narrow_taps, broad_taps))
    stream_table = jnp.asarray(
        np.transpose(filter_table(cells_x, narrow_taps, broad_taps), (1, 0, 2))
    )
    along_span = jnp.einsum("cpxz,zsn->cpxsn", widened, span_table, precision=lax.Precision.HIGHEST)
    filtered = jnp.einsum(
        "cpxsn,sxm->scpmn", along_span, stream_table, precision=lax.Precision.HIGHEST
    )
    narrow = filtered[0]
    broader = filtered[1]
    narrow_set = narrow.astype(jnp.bfloat16).reshape(chan_dev, row_count)
    broad_set = (
        (broader * root_weight[None, :, None, None])
        .astype(jnp.bfloat16)
        .reshape(chan_dev, row_count)
    )
    weighted = (stresses.astype(jnp.float32) * root_weight[None, :, None, None]).astype(
        jnp.bfloat16
    )
    weighted = weighted.reshape(STRESS, row_count)
    block_rows = math.gcd(row_count, 4096)
    block_count = row_count // block_rows
    narrow_all, broad_all = (
        lax.all_gather(narrow_set, "cols", axis=0, tiled=True),
        lax.all_gather(broad_set, "cols", axis=0, tiled=True),
    )

    def gram_step(block_index, carry):
        gram_acc, rhs_acc = carry
        start = block_index * block_rows
        narrow_piece = lax.dynamic_slice_in_dim(narrow_all, start, block_rows, 1)
        broad_piece = lax.dynamic_slice_in_dim(broad_all, start, block_rows, 1)
        own_piece = lax.dynamic_slice_in_dim(narrow_set, start, block_rows, 1)
        all_terms = library(narrow_piece, broad_piece)
        own_terms = library(own_piece, broad_piece)
        weighted_piece = lax.dynamic_slice_in_dim(weighted, start, block_rows, 1)
        gram_acc = gram_acc + jnp.einsum(
            "ir,jr->ij", own_terms, all_terms, preferred_element_type=jnp.float32
        )
        rhs_acc = rhs_acc + jnp.einsum(
            "ir,kr->ik", own_terms, weighted_piece, preferred_element_type=jnp.float32
        )
        return (gram_acc, rhs_acc)

    gram_block, rhs_block = lax.fori_loop(
        0,
        block_count,
        gram_step,
        (jnp.zeros((term_dev, TERMS), jnp.float32), jnp.zeros((term_dev, STRESS), jnp.float32)),
    )
    gram_block, rhs_block = lax.psum((gram_block, rhs_block), ("slab", "rep"))
    diag_own = jnp.diagonal(lax.dynamic_slice_in_dim(gram_block, offset, term_dev, 1))
    diag_all, rhs_all = (
        lax.all_gather(diag_own, "cols", axis=0, tiled=True),
        lax.all_gather(rhs_block, "cols", axis=0, tiled=True),
    )
    column_scale = 1.0 / jnp.sqrt(diag_all / samples + epsilon)
    scale_own = lax.dynamic_slice_in_dim(column_scale, offset, term_dev, 0)
    normal_rows = scale_own[:, None] * gram_block * column_scale[None, :] / samples
    target_norm = column_scale[None, :] * rhs_all.T / samples
    results = []

    def apply_pieces(vector_own, active_own):
        gathered = lax.all_gather(active_own * vector_own, "cols", axis=1, tiled=True)
        product = jnp.einsum("kl,il->ki", gathered, normal_rows, precision=lax.Precision.HIGHEST)
        return active_own * product + ridge_weight * vector_own

    def norm_of(vector_own):
        return lax.psum(jnp.sum(vector_own * vector_own, axis=1), "cols")

    target_own = lax.dynamic_slice_in_dim(target_norm, offset, term_dev, 1)
    solution_own = jnp.zeros((STRESS, term_dev), jnp.float32)
    for pass_index in range(PASSES):
        active_own = lax.dynamic_slice_in_dim(
            active_masks[pass_index].astype(jnp.float32), offset, term_dev, 1
        )
        solution_own = active_own * solution_own
        remain = active_own * target_own - apply_pieces(solution_own, active_own)
        direction = remain
        norm_now = norm_of(remain)
        for turn_index in range(ITERS):
            applied = apply_pieces(direction, active_own)
            curve_sum = lax.psum(jnp.sum(direction * applied, axis=1), "cols")
            step_size = norm_now / (curve_sum + epsilon)
            solution_own = solution_own + step_size[:, None] * direction
            remain = remain - step_size[:, None] * applied
            norm_next = norm_of(remain)
            direction = remain + (norm_next / (norm_now + epsilon))[:, None] * direction
            norm_now = norm_next
        results.append(solution_own)
    final_solution = lax.all_gather(solution_own, "cols", axis=1, tiled=True)
    coefficients = jnp.stack(results)
    final_weights = (column_scale[None, :] * final_solution).astype(jnp.bfloat16)

    def misfit_step(block_index, misfit_acc):
        start = block_index * block_rows
        narrow_piece = lax.dynamic_slice_in_dim(narrow_all, start, block_rows, 1)
        broad_piece = lax.dynamic_slice_in_dim(broad_all, start, block_rows, 1)
        all_terms = library(narrow_piece, broad_piece)
        predicted = jnp.dot(final_weights, all_terms, preferred_element_type=jnp.float32)
        weighted_piece = lax.dynamic_slice_in_dim(weighted, start, block_rows, 1)
        piece_misfit = (weighted_piece.astype(jnp.float32) - predicted).astype(jnp.bfloat16)
        return lax.dynamic_update_slice_in_dim(misfit_acc, piece_misfit, start, 1)

    misfit = lax.fori_loop(
        0, block_count, misfit_step, jnp.zeros((STRESS, row_count), jnp.bfloat16)
    )
    misfit = misfit.reshape(STRESS, plane_count, coarse_x, coarse_z)
    return (coefficients, misfit)


def solution(mesh):
    placed = (
        P("cols", "groups", "rep", "slab"),
        P(None, "groups", "rep", "slab"),
        P("groups"),
        P(),
    )
    return jax.shard_map(
        local,
        mesh=mesh,
        in_specs=placed,
        out_specs=(P(None, "groups", "cols"), P(None, "groups", "rep", "slab")),
        check_vma=False,
    )
```

profile of v0, /device:TPU:0, one launch (start us, length us, event | category | flops | bytes accessed | tf_op | source)
XLA Modules:
  0.0 648.6 jit_solution(8364757962872632828)
XLA Ops:
  7.2 11.5 %copy.51 = bf16[4,4,1024,256]{2,3,1,0:T(8,128)(2,1)} copy(bf16[4,4,1024,256]{3,2,1,0:T(8,128)(2,1)} %param.10) | data formatting | bytes 16777216 | tf_op args[0]
  47.7 18.5 %concatenate.11 = bf16[4,4,1034,266]{2,3,1,0:T(8,128)(2,1)} concatenate(bf16[4,4,5,266]{2,3,1,0:T(8,128)(2,1)S(1)} %copy.56, bf16[4,4,1024,266]{2,3,1,0:T(8,128)(2,1)} %copy-done, bf16[4,4,5,266]{2,3,1,0:T(8,128)(2,1)S(1)} %copy.57), dimensions={2} | concatenate | bytes 17602816 | tf_op jit(solution)/shard_map/concatenate | solution.py:26
  66.2 10.5 %fusion.5 = f32[4,4,1034,2,64]{2,4,1,0,3:T(8,128)S(1)} fusion(f32[266,2,64,1,1]{0,2,4,3,1:T(8,128)S(1)} %copy-done.5, bf16[4,4,1034,266]{2,3,1,0:T(8,128)(2,1)} %concatenate.11), kind=kOutput, calls=%fused_computation.17 | convolution fusion | flops 6759481344 | bytes 17408128 | tf_op jit(solution)/shard_map/cpxz,zsn->cpxsn/dot_general | solution.py:75
  97.4 39.6 %all-gather.19.cloned.1.call-done = bf16[4,4,65536]{2,1,0:T(4,128)(2,1)} async-done(((bf16[1,4,65536]{2,1,0:T(4,128)(2,1)}), bf16[4,4,65536]{2,1,0:T(4,128)(2,1)}) %all-gather.19.cloned.1.call-update) | async-done | bytes 2097168 | tf_op jit(solution)/shard_map/all_gather | solution.py:95
  139.9 43.4 %all-gather.21.cloned.1.call-done = bf16[4,4,65536]{2,1,0:T(4,128)(2,1)} async-done(((bf16[1,4,65536]{2,1,0:T(4,128)(2,1)}), bf16[4,4,65536]{2,1,0:T(4,128)(2,1)}) %all-gather.21.cloned.1.call-update) | async-done | bytes 2097168 | tf_op jit(solution)/shard_map/all_gather | solution.py:94
  186.1 53.2 %while.30 = (s32[]{:T(128)}, f32[64,256]{1,0:T(8,128)S(1)}, f32[64,6]{0,1:T(8,128)S(1)}, bf16[4,65536]{1,0:T(4,128)(2,1)S(1)}, bf16[16,65536]{1,0:T(8,128)(2,1)}...) while((s32[]{:T(128)}, f32[64,256]{1,0:T(8,128)S(1)}, ...), condition=%wide.region_1.0_spmd.clone, body=%wide.region_0.0_spmd.clone.sunk | while | flops 140165888 | bytes 7703730 | solution.py:115
  240.0 13.1 %all-gather.3 = f32[4,64,6]{1,2,0:T(8,128)S(1)} all-gather(f32[1,64,6]{1,2,0:T(8,128)S(1)} %fusion.29), channel_id=1, replica_groups=mesh['groups'=2,'cols'=4,'slab'=2,'rep'=2] {'cols'}, dimensions={0}, use_global_device_ids=true | all-gather | bytes 7680 | tf_op jit(solution)/shard_map/all_gather | solution.py:134
  260.1 13.1 %all-gather.2 = f32[4,64,6]{1,2,0:T(8,128)S(1)} all-gather(f32[1,64,6]{1,2,0:T(8,128)S(1)} %bitcast.248), channel_id=1, replica_groups=mesh['groups'=2,'cols'=4,'slab'=2,'rep'=2] {'cols'}, dimensions={0}, use_global_device_ids=true | all-gather | bytes 7680 | tf_op jit(solution)/shard_map/all_gather | solution.py:125
  286.0 13.1 %all-gather.4 = f32[4,64,6]{1,2,0:T(8,128)S(1)} all-gather(f32[1,64,6]{1,2,0:T(8,128)S(1)} %multiply_bitcast_fusion.10), channel_id=1, replica_groups=mesh['groups'=2,'cols'=4,'slab'=2,'rep'=2] {'cols'}, dimensions={0}, use_global_device_ids=true | all-gather | bytes 7680 | tf_op jit(solution)/shard_map/all_gather | solution.py:134
  319.5 13.1 %all-gather.5 = f32[4,64,6]{1,2,0:T(8,128)S(1)} all-gather(f32[1,64,6]{1,2,0:T(8,128)S(1)} %get-tuple-element.325), channel_id=1, replica_groups=mesh['groups'=2,'cols'=4,'slab'=2,'rep'=2] {'cols'}, dimensions={0}, use_global_device_ids=true | all-gather | bytes 7680 | tf_op jit(solution)/shard_map/all_gather | solution.py:134
  352.9 13.1 %all-gather.6 = f32[4,64,6]{1,2,0:T(8,128)S(1)} all-gather(f32[1,64,6]{1,2,0:T(8,128)S(1)} %get-tuple-element.323), channel_id=1, replica_groups=mesh['groups'=2,'cols'=4,'slab'=2,'rep'=2] {'cols'}, dimensions={0}, use_global_device_ids=true | all-gather | bytes 7680 | tf_op jit(solution)/shard_map/all_gather | solution.py:134
  376.7 13.1 %all-gather.7 = f32[4,64,6]{1,2,0:T(8,128)S(1)} all-gather(f32[1,64,6]{1,2,0:T(8,128)S(1)} %get-tuple-element.321), channel_id=1, replica_groups=mesh['groups'=2,'cols'=4,'slab'=2,'rep'=2] {'cols'}, dimensions={0}, use_global_device_ids=true | all-gather | bytes 7680 | tf_op jit(solution)/shard_map/all_gather | solution.py:134
  391.1 13.1 %all-gather.8 = f32[4,64,6]{1,2,0:T(8,128)S(1)} all-gather(f32[1,64,6]{1,2,0:T(8,128)S(1)} %multiply_bitcast_fusion.6), channel_id=1, replica_groups=mesh['groups'=2,'cols'=4,'slab'=2,'rep'=2] {'cols'}, dimensions={0}, use_global_device_ids=true | all-gather | bytes 7680 | tf_op jit(solution)/shard_map/all_gather | solution.py:134
  405.5 9.5 %all-reduce.2 = (f32[6]{0:T(128)S(1)}, f32[6]{0:T(128)S(1)}) all-reduce(f32[6]{0:T(128)S(1)} %get-tuple-element.272, f32[6]{0:T(128)S(1)} %get-tuple-element.271), channel_id=1, replica_groups=mesh['groups'=2,'cols'=4,'slab'=2,'rep'=2] {'cols'}, use_global_device_ids=true, to_apply=%region_17.18 | all-reduce | flops 12 | bytes 96 | tf_op jit(solution)/shard_map/psum | solution.py:139
  424.5 13.1 %all-gather.9 = f32[4,64,6]{1,2,0:T(8,128)S(1)} all-gather(f32[1,64,6]{1,2,0:T(8,128)S(1)} %get-tuple-element.317), channel_id=1, replica_groups=mesh['groups'=2,'cols'=4,'slab'=2,'rep'=2] {'cols'}, dimensions={0}, use_global_device_ids=true | all-gather | bytes 7680 | tf_op jit(solution)/shard_map/all_gather | solution.py:134
  438.9 9.5 %psum.151 = f32[6]{0:T(128)S(1)} all-reduce(f32[6]{0:T(128)S(1)} %get-tuple-element.344), channel_id=1, replica_groups=mesh['groups'=2,'cols'=4,'slab'=2,'rep'=2] {'cols'}, use_global_device_ids=true, to_apply=%region_23.24 | all-reduce | flops 6 | bytes 48 | tf_op jit(solution)/shard_map/psum | solution.py:153
  458.0 13.1 %all-gather.10 = f32[4,64,6]{1,2,0:T(8,128)S(1)} all-gather(f32[1,64,6]{1,2,0:T(8,128)S(1)} %get-tuple-element.315), channel_id=1, replica_groups=mesh['groups'=2,'cols'=4,'slab'=2,'rep'=2] {'cols'}, dimensions={0}, use_global_device_ids=true | all-gather | bytes 7680 | tf_op jit(solution)/shard_map/all_gather | solution.py:134
  472.4 9.5 %psum.153 = f32[6]{0:T(128)S(1)} all-reduce(f32[6]{0:T(128)S(1)} %fusion.26), channel_id=1, replica_groups=mesh['groups'=2,'cols'=4,'slab'=2,'rep'=2] {'cols'}, use_global_device_ids=true, to_apply=%region_27.28 | all-reduce | flops 6 | bytes 48 | tf_op jit(solution)/shard_map/psum | solution.py:153
  482.0 13.1 %all-gather.11 = f32[4,64,6]{1,2,0:T(8,128)S(1)} all-gather(f32[1,64,6]{1,2,0:T(8,128)S(1)} %get-tuple-element.313), channel_id=1, replica_groups=mesh['groups'=2,'cols'=4,'slab'=2,'rep'=2] {'cols'}, dimensions={0}, use_global_device_ids=true | all-gather | bytes 7680 | tf_op jit(solution)/shard_map/all_gather | solution.py:134
  495.5 13.1 %all-gather.12 = f32[4,64,6]{1,2,0:T(8,128)S(1)} all-gather(f32[1,64,6]{1,2,0:T(8,128)S(1)} %multiply_bitcast_fusion.2), channel_id=1, replica_groups=mesh['groups'=2,'cols'=4,'slab'=2,'rep'=2] {'cols'}, dimensions={0}, use_global_device_ids=true | all-gather | bytes 7680 | tf_op jit(solution)/shard_map/all_gather | solution.py:134
  528.1 13.1 %all-gather.13 = f32[4,64,6]{1,2,0:T(8,128)S(1)} all-gather(f32[1,64,6]{1,2,0:T(8,128)S(1)} %get-tuple-element.309), channel_id=1, replica_groups=mesh['groups'=2,'cols'=4,'slab'=2,'rep'=2] {'cols'}, dimensions={0}, use_global_device_ids=true | all-gather | bytes 7680 | tf_op jit(solution)/shard_map/all_gather | solution.py:134
  560.7 13.1 %all-gather.14 = f32[4,64,6]{1,2,0:T(8,128)S(1)} all-gather(f32[1,64,6]{1,2,0:T(8,128)S(1)} %get-tuple-element.307), channel_id=1, replica_groups=mesh['groups'=2,'cols'=4,'slab'=2,'rep'=2] {'cols'}, dimensions={0}, use_global_device_ids=true | all-gather | bytes 7680 | tf_op jit(solution)/shard_map/all_gather | solution.py:134
  583.6 13.4 %all-gather.15 = f32[4,64,6]{1,2,0:T(8,128)S(1)} all-gather(f32[1,64,6]{1,2,0:T(8,128)S(1)} %bitcast.246), channel_id=1, replica_groups=mesh['groups'=2,'cols'=4,'slab'=2,'rep'=2] {'cols'}, dimensions={0}, use_global_device_ids=true | all-gather | bytes 7680 | tf_op jit(solution)/shard_map/all_gather | solution.py:161
  597.2 41.2 %while.29 = (s32[]{:T(128)}, bf16[6,65536]{1,0:T(8,128)(2,1)S(1)}, bf16[6,65536]{1,0:T(8,128)(2,1)}, bf16[16,65536]{1,0:T(8,128)(2,1)}, bf16[16,65536]{1,0:T(8,1...) while((s32[]{:T(128)}, bf16[6,65536]{1,0:T(8,128)(2,1)S(1)}, ...), condition=%wide.region_41.42_spmd, body=%wide.region_40.41_spmd.sunk | while | flops 14884870 | bytes 5623963 | solution.py:175
  (307 shorter events, 296.9 us)
Async XLA Ops:
  7.2 129.9 %all-gather.19.cloned.1.call-start = ((), (), s32[]{:S(2)}) async-start(), calls=%async_computation.1 | async-start | bytes 2621440 | tf_op jit(solution)/shard_map/all_gather | solution.py:95
  19.8 10.1 %collective-permute-start = (bf16[4,4,1024,5]{2,3,1,0:T(8,128)(2,1)S(1)}, bf16[4,4,1024,5]{2,3,1,0:T(8,128)(2,1)S(1)}, u32[]{:S(2)}, u32[]{:S(2)}) collective-permute-start(bf16[4,4,1024,5]{2,3,1,0:T(8,128)(2,1)S(1)} %get-tuple-element.335), channel_id=1, source_target_pairs={{0,2},{2,0},{1,3},{3,1},{4,6},{6,4},{5,7},{7,5},{8,10},{10,8},{9,1... | collective-permute-start | bytes 491528 | tf_op jit(solution)/shard_map/ppermute | solution.py:24
  22.8 11.9 %collective-permute-start.1 = (bf16[4,4,1024,5]{2,3,1,0:T(8,128)(2,1)S(1)}, bf16[4,4,1024,5]{2,3,1,0:T(8,128)(2,1)S(1)}, u32[]{:S(2)}, u32[]{:S(2)}) collective-permute-start(bf16[4,4,1024,5]{2,3,1,0:T(8,128)(2,1)S(1)} %get-tuple-element.336), channel_id=1, source_target_pairs={{2,0},{0,2},{3,1},{1,3},{6,4},{4,6},{7,5},{5,7},{10,8},{8,10},{11,... | collective-permute-start | bytes 491528 | tf_op jit(solution)/shard_map/ppermute | solution.py:25
  40.3 3.5 copy-start
  44.4 1.8 copy-start.8
  45.0 1.5 collective-permute-start.2
  45.6 1.5 collective-permute-start.3
  47.7 18.5 %copy-start.5 = (f32[266,2,64,1,1]{0,2,4,3,1:T(8,128)S(1)}, f32[266,2,64,1,1]{0,2,4,3,1:T(8,128)}, u32[]{:S(2)}) copy-start(f32[266,2,64,1,1]{0,2,4,3,1:T(8,128)} %constant.133) | copy-start | bytes 408580
  66.2 10.5 %copy-start.3 = (f32[2,1034,256,1,1]{2,1,4,3,0:T(8,128)S(1)}, f32[2,1034,256,1,1]{2,1,4,3,0:T(8,128)}, u32[]{:S(2)}) copy-start(f32[2,1034,256,1,1]{2,1,4,3,0:T(8,128)} %constant.134) | copy-start | bytes 6352900
  85.4 1.4 copy-start.1
  89.4 3.7 copy-start.4
  89.4 93.9 %all-gather.21.cloned.1.call-start = ((), (), s32[]{:S(2)}) async-start(), calls=%async_computation.2 | async-start | bytes 2621440 | tf_op jit(solution)/shard_map/all_gather | solution.py:94
  92.8 180.5 %all-reduce.6.cloned.1.call-start = ((), (), s32[]{:S(2)}) async-start(), calls=%async_computation | async-start | bytes 131072 | tf_op jit(solution)/shard_map/psum | solution.py:121
  93.5 3.2 copy-start.6
  186.1 67.1 %copy-start.9 = (u32[32]{0:T(128)S(1)}, u32[32]{0:T(128)}, u32[]{:S(2)}) copy-start(u32[32]{0:T(128)} %constant.129) | copy-start | bytes 388
  239.3 0.6 copy-start.2
  273.4 221.9 %copy-start.7 = (f32[64,256]{1,0:T(8,128)S(1)}, f32[64,256]{1,0:T(8,128)}, u32[]{:S(2)}) copy-start(f32[64,256]{1,0:T(8,128)} %all-reduce.6.cloned.1.call-done) | copy-start | bytes 196612
Sparse Core Ops, SparseCore 0:
  89.5 47.4 all-gather.18
  138.6 44.6 all-gather.20
  240.1 29.7 all-reduce.5
where the time goes:
time: 652 us; the launch traced here: 649 us
  blocking collectives  340 us (52%)
  waiting for transfers between devices  94.9 us (15%)
  matrix products  79.3 us (12%)
  local copies, waits for them, and re-layouts  61 us (9%)
  other arithmetic  54.1 us (8%)
  between operations  14.7 us (2%)
    all_gather x12, blocking collectives, apply_pieces(): lax.all_gather(active_own * vector_own, 'cols', axis=1, tiled=True)  158 us
    psum x9, blocking collectives, norm_of(): return lax.psum(jnp.sum(vector_own * vector_own, axis=1), 'cols')  84.5 us
    psum x6, blocking collectives, local(): curve_sum = lax.psum(jnp.sum(direction * applied, axis=1), 'cols')  56.1 us
    all_gather x1, waiting for transfers between devices, local(): lax.all_gather(narrow_set, 'cols', axis=0, tiled=True)  43.4 us
    all_gather x1, waiting for transfers between devices, local(): lax.all_gather(broad_set, 'cols', axis=0, tiled=True)  39.6 us
    unnamed x42, local copies, waits for them, and re-layouts  27.5 us
    dot_general x16, matrix products, misfit_step(): jnp.dot(final_weights, all_terms, preferred_element_type=jnp.float32)  19.7 us
    concatenate x1, local copies, waits for them, and re-layouts, extended(): array = jnp.concatenate([before, array, after], axis=dim)  18.5 us
  transfers between devices with their start and end apart: 7, of which 4 were waited for; matrix products, arithmetic and copies ran while one was open for 2% of the time, Pallas kernels for 0%

commit v1 on v0

--- a/solution.py
+++ b/solution.py
@@ -1,3 +1,4 @@
+import functools
 import math
 import jax
 import jax.numpy as jnp
@@ -12,6 +13,22 @@
 ITERS = 3
 ridge_weight = 0.05
 epsilon = 1e-06
+
+
+def choose_roots_on_mesh(vec, shard_axis):
+    num = lax.axis_size(shard_axis)
+    by_place = [(h, (h + 1) % num) for h in range(num)]
+    runs = [(h, (h - 1) % num) for h in range(num)]
+    s_next, frame_out = ([vec], [vec])
+    for _ in range(num // 2):
+        s_next.append(lax.ppermute(s_next[-1], shard_axis, by_place))
+    for _ in [*range((num - 1) // 2)]:
+        frame_out.append(lax.ppermute(frame_out[-1], shard_axis, runs))
+    outer = jnp.concatenate([*s_next[::-1], *frame_out[1:]], axis=0)
+    return jnp.roll(outer, (lax.axis_index(shard_axis) - num // 2) * vec.shape[0], axis=0)
+
+
+switch_marks_in = functools.partial(choose_roots_on_mesh, shard_axis="cols")
 
 
 def extended(array, sides, width):
@@ -122,7 +139,7 @@
     diag_own = jnp.diagonal(lax.dynamic_slice_in_dim(gram_block, offset, term_dev, 1))
     diag_all, rhs_all = (
         lax.all_gather(diag_own, "cols", axis=0, tiled=True),
-        lax.all_gather(rhs_block, "cols", axis=0, tiled=True),
+        switch_marks_in(rhs_block),
     )
     column_scale = 1.0 / jnp.sqrt(diag_all / samples + epsilon)
     scale_own = lax.dynamic_slice_in_dim(column_scale, offset, term_dev, 0)

time: 652 us -> 650 us (level)
  blocking collectives: 340 us -> 329 us
    all_gather x1 -> x0, blocking collectives: 13.1 us -> none  [local(): lax.all_gather(rhs_block, 'cols', axis=0, tiled=True)]
    unnamed x42 -> x41, local copies, waits for them, and re-layouts: 27.5 us -> 27.4 us
  transfers between devices with their start and end apart: 7 -> 10, of which waited for: 4 -> 6; matrix products, arithmetic and copies ran while one was open for 2% -> 2% of each run, Pallas kernels for 0% -> 0%
where the time goes in v1:
time: 650 us; the launch traced here: 646 us
  blocking collectives  329 us (51%)
  waiting for transfers between devices  99.6 us (15%)
  matrix products  79.3 us (12%)
  local copies, waits for them, and re-layouts  61 us (9%)
  other arithmetic  54.1 us (8%)
  between operations  14.8 us (2%)
  starting transfers between devices  7.9 us (1%)
    all_gather x12, blocking collectives, apply_pieces(): lax.all_gather(active_own * vector_own, 'cols', axis=1, tiled=True)  157 us
    psum x9, blocking collectives, norm_of(): return lax.psum(jnp.sum(vector_own * vector_own, axis=1), 'cols')  85.4 us
    psum x6, blocking collectives, local(): curve_sum = lax.psum(jnp.sum(direction * applied, axis=1), 'cols')  54.3 us
    all_gather x1, waiting for transfers between devices, local(): lax.all_gather(narrow_set, 'cols', axis=0, tiled=True)  43.4 us
    all_gather x1, waiting for transfers between devices, local(): lax.all_gather(broad_set, 'cols', axis=0, tiled=True)  39.6 us
    unnamed x41, local copies, waits for them, and re-layouts  27.4 us
    dot_general x16, matrix products, misfit_step(): jnp.dot(final_weights, all_terms, preferred_element_type=jnp.float32)  19.7 us
    concatenate x1, local copies, waits for them, and re-layouts, extended(): array = jnp.concatenate([before, array, after], axis=dim)  18.5 us
  transfers between devices with their start and end apart: 10, of which 6 were waited for; matrix products, arithmetic and copies ran while one was open for 2% of the time, Pallas kernels for 0%

profile of v1, /device:TPU:0, one launch (start us, length us, event | category | flops | bytes accessed | tf_op | source)
XLA Modules:
  0.0 646.4 jit_solution(5297748772696625126)
XLA Ops:
  7.2 11.5 %copy.48 = bf16[4,4,1024,256]{2,3,1,0:T(8,128)(2,1)} copy(bf16[4,4,1024,256]{3,2,1,0:T(8,128)(2,1)} %param.10) | data formatting | bytes 16777216 | tf_op args[0]
  47.7 18.5 %concatenate.17 = bf16[4,4,1034,266]{2,3,1,0:T(8,128)(2,1)} concatenate(bf16[4,4,5,266]{2,3,1,0:T(8,128)(2,1)S(1)} %copy.53, bf16[4,4,1024,266]{2,3,1,0:T(8,128)(2,1)} %copy-done, bf16[4,4,5,266]{2,3,1,0:T(8,128)(2,1)S(1)} %copy.54), dimensions={2} | concatenate | bytes 17602816 | tf_op jit(solution)/shard_map/concatenate | solution.py:43
  66.2 10.5 %fusion.5 = f32[4,4,1034,2,64]{2,4,1,0,3:T(8,128)S(1)} fusion(f32[266,2,64,1,1]{0,2,4,3,1:T(8,128)S(1)} %copy-done.5, bf16[4,4,1034,266]{2,3,1,0:T(8,128)(2,1)} %concatenate.17), kind=kOutput, calls=%fused_computation.17 | convolution fusion | flops 6759481344 | bytes 17408128 | tf_op jit(solution)/shard_map/cpxz,zsn->cpxsn/dot_general | solution.py:92
  97.4 39.6 %all-gather.18.cloned.1.call-done = bf16[4,4,65536]{2,1,0:T(4,128)(2,1)} async-done(((bf16[1,4,65536]{2,1,0:T(4,128)(2,1)}), bf16[4,4,65536]{2,1,0:T(4,128)(2,1)}) %all-gather.18.cloned.1.call-update) | async-done | bytes 2097168 | tf_op jit(solution)/shard_map/all_gather | solution.py:112
  139.9 43.4 %all-gather.20.cloned.1.call-done = bf16[4,4,65536]{2,1,0:T(4,128)(2,1)} async-done(((bf16[1,4,65536]{2,1,0:T(4,128)(2,1)}), bf16[4,4,65536]{2,1,0:T(4,128)(2,1)}) %all-gather.20.cloned.1.call-update) | async-done | bytes 2097168 | tf_op jit(solution)/shard_map/all_gather | solution.py:111
  186.1 53.2 %while.30 = (s32[]{:T(128)}, f32[64,256]{1,0:T(8,128)S(1)}, f32[64,6]{0,1:T(8,128)S(1)}, bf16[4,65536]{1,0:T(4,128)(2,1)S(1)}, bf16[16,65536]{1,0:T(8,128)(2,1)}...) while((s32[]{:T(128)}, f32[64,256]{1,0:T(8,128)S(1)}, ...), condition=%wide.region_1.0_spmd.clone, body=%wide.region_0.0_spmd.clone.sunk | while | flops 140165888 | bytes 7703730 | solution.py:132
  247.0 13.1 %all-gather.2 = f32[4,64,6]{1,2,0:T(8,128)S(1)} all-gather(f32[1,64,6]{1,2,0:T(8,128)S(1)} %fusion.29), channel_id=1, replica_groups=mesh['groups'=2,'cols'=4,'slab'=2,'rep'=2] {'cols'}, dimensions={0}, use_global_device_ids=true | all-gather | bytes 7680 | tf_op jit(solution)/shard_map/all_gather | solution.py:151
  271.9 11.6 %all-reduce = f32[256]{0:T(256)S(1)} all-reduce(f32[256]{0:T(256)S(1)} %dynamic-update-slice), channel_id=1, replica_groups=mesh['groups'=2,'cols'=4,'slab'=2,'rep'=2] {'cols'}, use_global_device_ids=true, to_apply=%add | all-reduce | flops 256 | bytes 2048
  284.8 13.1 %all-gather.3 = f32[4,64,6]{1,2,0:T(8,128)S(1)} all-gather(f32[1,64,6]{1,2,0:T(8,128)S(1)} %multiply_bitcast_fusion.10), channel_id=1, replica_groups=mesh['groups'=2,'cols'=4,'slab'=2,'rep'=2] {'cols'}, dimensions={0}, use_global_device_ids=true | all-gather | bytes 7680 | tf_op jit(solution)/shard_map/all_gather | solution.py:151
  307.8 10.4 %psum.144 = f32[6]{0:T(128)S(1)} all-reduce(f32[6]{0:T(128)S(1)} %get-tuple-element.327), channel_id=1, replica_groups=mesh['groups'=2,'cols'=4,'slab'=2,'rep'=2] {'cols'}, use_global_device_ids=true, to_apply=%region_9.10 | all-reduce | flops 6 | bytes 48 | tf_op jit(solution)/shard_map/psum | solution.py:156
  318.3 13.1 %all-gather.4 = f32[4,64,6]{1,2,0:T(8,128)S(1)} all-gather(f32[1,64,6]{1,2,0:T(8,128)S(1)} %get-tuple-element.325), channel_id=1, replica_groups=mesh['groups'=2,'cols'=4,'slab'=2,'rep'=2] {'cols'}, dimensions={0}, use_global_device_ids=true | all-gather | bytes 7680 | tf_op jit(solution)/shard_map/all_gather | solution.py:151
  351.7 13.1 %all-gather.5 = f32[4,64,6]{1,2,0:T(8,128)S(1)} all-gather(f32[1,64,6]{1,2,0:T(8,128)S(1)} %get-tuple-element.323), channel_id=1, replica_groups=mesh['groups'=2,'cols'=4,'slab'=2,'rep'=2] {'cols'}, dimensions={0}, use_global_device_ids=true | all-gather | bytes 7680 | tf_op jit(solution)/shard_map/all_gather | solution.py:151
  374.6 13.1 %all-gather.6 = f32[4,64,6]{1,2,0:T(8,128)S(1)} all-gather(f32[1,64,6]{1,2,0:T(8,128)S(1)} %get-tuple-element.321), channel_id=1, replica_groups=mesh['groups'=2,'cols'=4,'slab'=2,'rep'=2] {'cols'}, dimensions={0}, use_global_device_ids=true | all-gather | bytes 7680 | tf_op jit(solution)/shard_map/all_gather | solution.py:151
  388.9 13.1 %all-gather.7 = f32[4,64,6]{1,2,0:T(8,128)S(1)} all-gather(f32[1,64,6]{1,2,0:T(8,128)S(1)} %multiply_bitcast_fusion.6), channel_id=1, replica_groups=mesh['groups'=2,'cols'=4,'slab'=2,'rep'=2] {'cols'}, dimensions={0}, use_global_device_ids=true | all-gather | bytes 7680 | tf_op jit(solution)/shard_map/all_gather | solution.py:151
  403.4 10.4 %all-reduce.2 = (f32[6]{0:T(128)S(1)}, f32[6]{0:T(128)S(1)}) all-reduce(f32[6]{0:T(128)S(1)} %get-tuple-element.272, f32[6]{0:T(128)S(1)} %get-tuple-element.271), channel_id=1, replica_groups=mesh['groups'=2,'cols'=4,'slab'=2,'rep'=2] {'cols'}, use_global_device_ids=true, to_apply=%region_17.18 | all-reduce | flops 12 | bytes 96 | tf_op jit(solution)/shard_map/psum | solution.py:156
  422.4 13.1 %all-gather.8 = f32[4,64,6]{1,2,0:T(8,128)S(1)} all-gather(f32[1,64,6]{1,2,0:T(8,128)S(1)} %get-tuple-element.317), channel_id=1, replica_groups=mesh['groups'=2,'cols'=4,'slab'=2,'rep'=2] {'cols'}, dimensions={0}, use_global_device_ids=true | all-gather | bytes 7680 | tf_op jit(solution)/shard_map/all_gather | solution.py:151
  436.8 10.4 %psum.151 = f32[6]{0:T(128)S(1)} all-reduce(f32[6]{0:T(128)S(1)} %get-tuple-element.344), channel_id=1, replica_groups=mesh['groups'=2,'cols'=4,'slab'=2,'rep'=2] {'cols'}, use_global_device_ids=true, to_apply=%region_23.24 | all-reduce | flops 6 | bytes 48 | tf_op jit(solution)/shard_map/psum | solution.py:170
  455.9 13.1 %all-gather.9 = f32[4,64,6]{1,2,0:T(8,128)S(1)} all-gather(f32[1,64,6]{1,2,0:T(8,128)S(1)} %get-tuple-element.315), channel_id=1, replica_groups=mesh['groups'=2,'cols'=4,'slab'=2,'rep'=2] {'cols'}, dimensions={0}, use_global_device_ids=true | all-gather | bytes 7680 | tf_op jit(solution)/shard_map/all_gather | solution.py:151
  480.7 13.1 %all-gather.10 = f32[4,64,6]{1,2,0:T(8,128)S(1)} all-gather(f32[1,64,6]{1,2,0:T(8,128)S(1)} %get-tuple-element.313), channel_id=1, replica_groups=mesh['groups'=2,'cols'=4,'slab'=2,'rep'=2] {'cols'}, dimensions={0}, use_global_device_ids=true | all-gather | bytes 7680 | tf_op jit(solution)/shard_map/all_gather | solution.py:151
  494.3 13.1 %all-gather.11 = f32[4,64,6]{1,2,0:T(8,128)S(1)} all-gather(f32[1,64,6]{1,2,0:T(8,128)S(1)} %multiply_bitcast_fusion.2), channel_id=1, replica_groups=mesh['groups'=2,'cols'=4,'slab'=2,'rep'=2] {'cols'}, dimensions={0}, use_global_device_ids=true | all-gather | bytes 7680 | tf_op jit(solution)/shard_map/all_gather | solution.py:151
  526.9 13.1 %all-gather.12 = f32[4,64,6]{1,2,0:T(8,128)S(1)} all-gather(f32[1,64,6]{1,2,0:T(8,128)S(1)} %get-tuple-element.309), channel_id=1, replica_groups=mesh['groups'=2,'cols'=4,'slab'=2,'rep'=2] {'cols'}, dimensions={0}, use_global_device_ids=true | all-gather | bytes 7680 | tf_op jit(solution)/shard_map/all_gather | solution.py:151
  559.5 13.1 %all-gather.13 = f32[4,64,6]{1,2,0:T(8,128)S(1)} all-gather(f32[1,64,6]{1,2,0:T(8,128)S(1)} %get-tuple-element.307), channel_id=1, replica_groups=mesh['groups'=2,'cols'=4,'slab'=2,'rep'=2] {'cols'}, dimensions={0}, use_global_device_ids=true | all-gather | bytes 7680 | tf_op jit(solution)/shard_map/all_gather | solution.py:151
  581.5 13.4 %all-gather.14 = f32[4,64,6]{1,2,0:T(8,128)S(1)} all-gather(f32[1,64,6]{1,2,0:T(8,128)S(1)} %bitcast.243), channel_id=1, replica_groups=mesh['groups'=2,'cols'=4,'slab'=2,'rep'=2] {'cols'}, dimensions={0}, use_global_device_ids=true | all-gather | bytes 7680 | tf_op jit(solution)/shard_map/all_gather | solution.py:178
  595.1 41.2 %while.29 = (s32[]{:T(128)}, bf16[6,65536]{1,0:T(8,128)(2,1)S(1)}, bf16[6,65536]{1,0:T(8,128)(2,1)}, bf16[16,65536]{1,0:T(8,128)(2,1)}, bf16[16,65536]{1,0:T(8,1...) while((s32[]{:T(128)}, bf16[6,65536]{1,0:T(8,128)(2,1)S(1)}, ...), condition=%wide.region_41.42_spmd, body=%wide.region_40.41_spmd.sunk | while | flops 14884870 | bytes 5623963 | solution.py:192
  (311 shorter events, 293.8 us)
Async XLA Ops:
  7.2 129.9 %all-gather.18.cloned.1.call-start = ((), (), s32[]{:S(2)}) async-start(), calls=%async_computation.1 | async-start | bytes 2621440 | tf_op jit(solution)/shard_map/all_gather | solution.py:112
  19.8 10.1 %collective-permute-start = (bf16[4,4,1024,5]{2,3,1,0:T(8,128)(2,1)S(1)}, bf16[4,4,1024,5]{2,3,1,0:T(8,128)(2,1)S(1)}, u32[]{:S(2)}, u32[]{:S(2)}) collective-permute-start(bf16[4,4,1024,5]{2,3,1,0:T(8,128)(2,1)S(1)} %get-tuple-element.335), channel_id=1, source_target_pairs={{0,2},{2,0},{1,3},{3,1},{4,6},{6,4},{5,7},{7,5},{8,10},{10,8},{9,1... | collective-permute-start | bytes 491528 | tf_op jit(solution)/shard_map/ppermute | solution.py:41
  22.8 11.9 %collective-permute-start.1 = (bf16[4,4,1024,5]{2,3,1,0:T(8,128)(2,1)S(1)}, bf16[4,4,1024,5]{2,3,1,0:T(8,128)(2,1)S(1)}, u32[]{:S(2)}, u32[]{:S(2)}) collective-permute-start(bf16[4,4,1024,5]{2,3,1,0:T(8,128)(2,1)S(1)} %get-tuple-element.336), channel_id=1, source_target_pairs={{2,0},{0,2},{3,1},{1,3},{6,4},{4,6},{7,5},{5,7},{10,8},{8,10},{11,... | collective-permute-start | bytes 491528 | tf_op jit(solution)/shard_map/ppermute | solution.py:42
  40.3 3.5 copy-start
  44.4 1.8 copy-start.8
  45.0 1.5 collective-permute-start.2
  45.6 1.5 collective-permute-start.3
  47.7 18.5 %copy-start.5 = (f32[266,2,64,1,1]{0,2,4,3,1:T(8,128)S(1)}, f32[266,2,64,1,1]{0,2,4,3,1:T(8,128)}, u32[]{:S(2)}) copy-start(f32[266,2,64,1,1]{0,2,4,3,1:T(8,128)} %constant.156) | copy-start | bytes 408580
  66.2 10.5 %copy-start.3 = (f32[2,1034,256,1,1]{2,1,4,3,0:T(8,128)S(1)}, f32[2,1034,256,1,1]{2,1,4,3,0:T(8,128)}, u32[]{:S(2)}) copy-start(f32[2,1034,256,1,1]{2,1,4,3,0:T(8,128)} %constant.157) | copy-start | bytes 6352900
  85.4 1.4 copy-start.1
  89.4 3.7 copy-start.4
  89.4 93.9 %all-gather.20.cloned.1.call-start = ((), (), s32[]{:S(2)}) async-start(), calls=%async_computation.2 | async-start | bytes 2621440 | tf_op jit(solution)/shard_map/all_gather | solution.py:111
  92.8 177.1 %all-reduce.6.cloned.1.call-start = ((), (), s32[]{:S(2)}) async-start(), calls=%async_computation | async-start | bytes 131072 | tf_op jit(solution)/shard_map/psum | solution.py:138
  93.5 3.2 copy-start.6
  186.1 77.9 %copy-start.9 = (u32[32]{0:T(128)S(1)}, u32[32]{0:T(128)}, u32[]{:S(2)}) copy-start(u32[32]{0:T(128)} %constant.152) | copy-start | bytes 388
  239.3 0.6 copy-start.2
  246.9 17.0 %collective-permute-start.4 = (f32[64,6]{0,1:T(8,128)S(1)}, f32[64,6]{0,1:T(8,128)S(1)}, u32[]{:S(2)}, u32[]{:S(2)}) collective-permute-start(f32[64,6]{0,1:T(8,128)S(1)} %psum.141), channel_id=1, source_target_pairs={{0,4},{4,8},{8,12},{12,0},{1,5},{5,9},{9,13},{13,1},{2,6},{6,10},{... | collective-permute-start | bytes 4616 | tf_op jit(solution)/shard_map/ppermute | solution.py:24
  260.1 5.2 collective-permute-start.6
  263.9 5.4 collective-permute-start.5
  270.0 224.0 %copy-start.7 = (f32[64,256]{1,0:T(8,128)S(1)}, f32[64,256]{1,0:T(8,128)}, u32[]{:S(2)}) copy-start(f32[64,256]{1,0:T(8,128)} %all-reduce.6.cloned.1.call-done) | copy-start | bytes 196612
Sparse Core Ops, SparseCore 0:
  89.5 47.4 all-gather.17
  138.6 44.6 all-gather.19
  240.1 29.8 all-reduce.5
